TPU v7x, 512 devices: a whole 4x4x16 slice. The times are simulated.
512 devices in a mesh: wide: 64 (over x, z), narrow: 8 (over y, core).
Axes of the slice: x: 4, y: 4, z: 16, core: 2. Of those that a mesh axis runs over, the one named last changes fastest.
Arguments:
- tokens: bfloat16 [49152, 2048], P('wide', 'narrow'), may hold values from -6 to 6
- norm_gain: float32 [2048], replicated, may hold values from 0.1 to 1.9
- qkv_weight: bfloat16 [2048, 3, 2048], P('wide', None, 'narrow'), may hold values from -0.125 to 0.125
- out_weight: bfloat16 [2048, 2048], P('wide', 'narrow'), may hold values from -0.25 to 0.25
- cache_pool: bfloat16 [1536, 128, 2, 2048], P('wide', None, None, 'narrow'), may hold values from -400 to 400, as said below
- prefix_pool: bfloat16 [2048, 2, 2048], P('wide', None, 'narrow'), may hold values from -6 to 6
- page_table: int32 [64, 24], P('wide'), may hold values from 0 to 23, each once within a row
- cache_len: int32 [64], P('wide'), may hold values from 512 to 3072
- group_ids: int32 [64], P('wide'), may hold values from 0 to 7, as said below
- group_pages: int32 [16], replicated, may hold values from 0 to 15, each once
Outputs:
- branch_out: bfloat16 [49152, 2048], P('wide', 'narrow')
- new_pages: bfloat16 [49152, 2, 2048], P('wide', None, 'narrow')
Inputs may be any that keep to these rules, and one draw needn't show every extreme that they name: `page_table`: each row is a permutation of the 24 pages of that request. `group_ids`: each group has 8 requests. `group_pages`: a permutation of the prefix pool's pages. `cache_pool`: keys are stored already rotated.
All inputs are finite; a program needn't handle non-finite values.
Results may differ from a plain program's by a relative error of at most 0.0095.
The roundings to bfloat16 on the way count: a program that leaves them out, or rounds other values in their place, can miss the bound.
Values may be sent and summed in bfloat16 or wider, within the bound.
No kernel may reach another device: no remote copies, remote signals or barrier semaphores. Data moves between devices by JAX's collectives and lax.ppermute only.
A program may use at most 128 MiB of HBM per device.

v0:
```python
import jax
import jax.numpy as jnp
from jax import lax
from jax.sharding import PartitionSpec as P

HEAD_DIM = 64
ROT = 16
PAGE = 128
KB = 4
PPAGES = 2
NEGATIVE = -1e30


def rotary(vectors, positions):
    half_rot = ROT // 2
    frequency = 10000.0 ** (-(jnp.arange(half_rot, dtype=jnp.float32) * 2.0 / ROT))
    angles = positions.astype(jnp.float32)[:, None] * frequency[None, :]
    cos_part = jnp.concatenate([jnp.cos(angles), jnp.cos(angles)], axis=1)[:, None, :]
    sine_part = jnp.concatenate([jnp.sin(angles), jnp.sin(angles)], axis=1)[:, None, :]
    rotated_in = vectors[..., :ROT]
    turned = jnp.concatenate([-rotated_in[..., half_rot:], rotated_in[..., :half_rot]], axis=-1)
    return jnp.concatenate(
        [rotated_in * cos_part + turned * sine_part, vectors[..., ROT:]], axis=-1
    )


def attend(running, queries, keys, values, key_valid):
    row_max, weight_sum, weighted = running
    scores = jnp.einsum("qhd,khd->hqk", queries, keys, preferred_element_type=jnp.float32) * 0.125
    scores = jnp.where(key_valid[None], scores, NEGATIVE)
    new_max = jnp.maximum(row_max, jnp.max(scores, axis=2))
    expo = jnp.where(key_valid[None], jnp.exp(scores - new_max[:, :, None]), 0.0)
    factor = jnp.exp(row_max - new_max)
    weight_sum = weight_sum * factor + jnp.sum(expo, axis=2)
    update = jnp.einsum(
        "hqk,khd->qhd", expo.astype(jnp.bfloat16), values, preferred_element_type=jnp.float32
    )
    weighted = weighted * jnp.transpose(factor)[:, :, None] + update
    return (new_max, weight_sum, weighted)


def local(
    tokens,
    norm_gain,
    qkv_weight,
    out_weight,
    cache_pool,
    prefix_pool,
    page_table,
    cache_len,
    group_ids,
    group_pages,
):
    span_rows = tokens.shape[0]
    local_width = qkv_weight.shape[2]
    heads_here = local_width // HEAD_DIM
    gathered = lax.all_gather(tokens, "narrow", axis=1, tiled=True)
    widened = gathered.astype(jnp.float32)
    row_mean = jnp.mean(widened, axis=1, keepdims=True)
    centered = widened - row_mean
    variance = jnp.mean(centered * centered, axis=1, keepdims=True)
    normed = (centered * lax.rsqrt(variance + 1e-05) * norm_gain).astype(jnp.bfloat16)
    piece_rows = lax.all_gather(qkv_weight, "wide", axis=0, tiled=True)
    piece_count = piece_rows.shape[0]
    columns = normed
    projected = jnp.dot(
        columns,
        piece_rows.reshape(piece_count, 3 * local_width),
        preferred_element_type=jnp.float32,
    )
    projected = projected.reshape(span_rows, 3, heads_here, HEAD_DIM)
    length = cache_len[0]
    offset = jnp.arange(span_rows, dtype=jnp.int32)
    positions = PPAGES * PAGE + length + offset
    queries = rotary(projected[:, 0], positions).astype(jnp.bfloat16)
    keys = rotary(projected[:, 1], positions).astype(jnp.bfloat16)
    values = projected[:, 2].astype(jnp.bfloat16)
    new_pages = jnp.stack(
        [keys.reshape(span_rows, local_width), values.reshape(span_rows, local_width)], axis=1
    )
    initial = (
        jnp.full((heads_here, span_rows), NEGATIVE, jnp.float32),
        jnp.zeros((heads_here, span_rows), jnp.float32),
        jnp.zeros((span_rows, heads_here, HEAD_DIM), jnp.float32),
    )
    running = attend(initial, queries, keys, values, offset[:, None] >= offset[None, :])
    my_group = group_ids[0]
    prefix_whole = lax.all_gather(prefix_pool, "wide", axis=0, tiled=True)
    prefix_pages = prefix_whole.reshape(-1, PAGE, 2, heads_here, HEAD_DIM)
    chosen = lax.dynamic_slice_in_dim(group_pages, my_group * PPAGES, PPAGES)
    key_rows = jnp.take(prefix_pages, chosen, axis=0).reshape(
        PPAGES * PAGE, 2, heads_here, HEAD_DIM
    )
    running = attend(
        running,
        queries,
        key_rows[:, 0],
        key_rows[:, 1],
        jnp.ones((span_rows, PPAGES * PAGE), dtype=bool),
    )
    page_list = page_table[0]
    block_keys = KB * PAGE
    blocks = (length + block_keys - 1) // block_keys
    key_offset = jnp.arange(block_keys, dtype=jnp.int32)

    def cache_block(block_index, state_now):
        page_ids = lax.dynamic_slice_in_dim(page_list, block_index * KB, KB)
        key_rows = jnp.take(cache_pool, page_ids, axis=0).reshape(
            block_keys, 2, heads_here, HEAD_DIM
        )
        key_valid = jnp.broadcast_to(
            (block_index * block_keys + key_offset < length)[None, :], (span_rows, block_keys)
        )
        return attend(state_now, queries, key_rows[:, 0], key_rows[:, 1], key_valid)

    running = lax.fori_loop(0, blocks, cache_block, running)
    head_values = (
        (running[2] / jnp.transpose(running[1])[:, :, None])
        .astype(jnp.bfloat16)
        .reshape(span_rows, local_width)
    )
    all_heads = lax.all_gather(head_values, "narrow", axis=1, tiled=True)
    columns = all_heads
    branch_out = jnp.dot(
        columns,
        lax.all_gather(out_weight, "wide", axis=0, tiled=True),
        preferred_element_type=jnp.float32,
    )
    return (branch_out.astype(jnp.bfloat16), new_pages)


def solution(mesh):
    placed = (
        P("wide", "narrow"),
        P(),
        P("wide", None, "narrow"),
        P("wide", "narrow"),
        P("wide", None, None, "narrow"),
        P("wide", None, "narrow"),
        P("wide", None),
        P("wide"),
        P("wide"),
        P(),
    )
    return jax.shard_map(
        local,
        mesh=mesh,
        in_specs=placed,
        out_specs=(P("wide", "narrow"), P("wide", None, "narrow")),
        check_vma=False,
    )
```

profile of v0, /device:TPU:1, one launch (start us, length us, event | category | flops | bytes accessed | tf_op | source)
XLA Modules:
  0.0 524.0 jit_solution(7641525677525579463)
XLA Ops:
  7.2 0.7 all-gather.10.cloned.1.call-update
  7.9 0.7 all-gather.6.cloned.1.call-update
  8.7 0.7 all-gather.8.cloned.1.call-update
  9.4 0.5 all-gather.14.cloned.1.call-update
  10.7 1.0 iota_compare_fusion
  12.3 0.7 compare_and_fusion.1
  13.2 0.2 multiply_cosine_fusion
  13.4 134.0 %all-gather.10.cloned.1.call-done = bf16[2048,2,256]{2,1,0:T(2,128)(2,1)} async-done(((bf16[32,2,256]{2,1,0:T(2,128)(2,1)}), bf16[2048,2,256]{2,1,0:T(2,128)(2,1)}) %all-gather.10.cloned.1.call-update) | async-done | bytes 2097168 | tf_op jit(solution)/shard_map/all_gather | solution.py:88
  147.3 8.8 %reshape.131 = bf16[16,128,2,4,64]{4,3,2,1,0:T(4,128)(2,1)} reshape(bf16[2048,2,256]{2,1,0:T(2,128)(2,1)} %all-gather.10.cloned.1.call-done) | data formatting | bytes 4194304 | tf_op jit(solution)/shard_map/reshape | solution.py:89
  156.2 5.8 %copy.32 = bf16[16,128,2,4,64]{1,4,3,2,0:T(8,128)(2,1)S(1)} copy(bf16[16,128,2,4,64]{4,3,2,1,0:T(4,128)(2,1)} %reshape.131) | data formatting | bytes 4194304 | tf_op jit(solution)/shard_map/reshape | solution.py:89
  161.9 0.6 gather_fusion.1
  162.6 31.8 %all-gather.6.cloned.1.call-done = bf16[768,2048]{1,0:T(8,128)(2,1)} async-done(((bf16[768,256]{1,0:T(8,128)(2,1)}), bf16[768,2048]{1,0:T(8,128)(2,1)}) %all-gather.6.cloned.1.call-update) | async-done | bytes 3145744 | tf_op jit(solution)/shard_map/all_gather | solution.py:57
  194.4 2.5 convert_reduce_fusion
  197.0 2.8 fusion.27
  199.8 132.6 %all-gather.8.cloned.1.call-done = bf16[2048,3,256]{2,0,1:T(8,128)(2,1)} async-done(((bf16[32,3,256]{2,0,1:T(8,128)(2,1)}), bf16[2048,3,256]{2,0,1:T(8,128)(2,1)}) %all-gather.8.cloned.1.call-update) | async-done | bytes 3145744 | tf_op jit(solution)/shard_map/all_gather | solution.py:63
  332.4 4.7 copy.30
  337.1 4.6 fusion.34
  341.8 0.1 slice_bitcast_fusion.4
  342.1 0.6 multiply_reduce_fusion
  342.8 0.5 copy-done.1
  343.3 1.8 fusion.22
  345.1 2.3 fusion.26
  347.4 2.8 fusion.57
  350.2 0.5 fusion.40
  350.8 0.7 fusion.51
  351.5 21.3 %while.15 = (s32[]{:T(128)}, f32[4,768]{1,0:T(4,128)S(1)}, f32[4,768]{1,0:T(4,128)S(1)}, f32[768,4,64]{0,2,1:T(8,128)S(1)}, s32[]{:T(128)}, /*index=5*/s32[]{:T(...) while((s32[]{:T(128)}, f32[4,768]{1,0:T(4,128)S(1)}, ...), condition=%wide.region_9.10_spmd.clone, body=%wide.region_6.9_spmd.clone.sunk | while | flops 423767072 | bytes 25763612 | solution.py:116
  351.5 0.7 fusion.88
  352.4 3.5 gather_fusion
  355.9 0.8 copy.47
  356.7 0.2 gather.23
  357.0 1.4 bitcast_reduce_fusion.2
  358.4 2.0 fusion.90
  360.3 1.7 fusion.91
  362.1 0.7 fusion.88
  362.9 3.5 gather_fusion
  366.4 0.8 copy.47
  367.2 0.2 gather.23
  367.5 1.4 bitcast_reduce_fusion.2
  368.9 2.0 fusion.90
  370.9 1.7 fusion.91
  372.8 0.8 divide_convert_fusion
  373.6 1.2 slice.106
  374.8 0.6 copy.37
  375.5 0.6 copy.36
  376.1 2.7 pad_maximum_fusion
  378.8 90.2 %all-gather.14.cloned.1.call-done = bf16[2048,256]{1,0:T(8,128)(2,1)} async-done(((bf16[32,256]{1,0:T(8,128)(2,1)}), bf16[2048,256]{1,0:T(8,128)(2,1)}) %all-gather.14.cloned.1.call-update) | async-done | bytes 1048592 | tf_op jit(solution)/shard_map/all_gather | solution.py:126
  469.0 44.6 %all-gather.12.cloned.1.call-done = bf16[768,2048]{0,1:T(8,128)(2,1)} async-done(((bf16[768,256]{0,1:T(8,128)(2,1)}), bf16[768,2048]{0,1:T(8,128)(2,1)}) %all-gather.12.cloned.1.call-update) | async-done | bytes 3145744 | tf_op jit(solution)/shard_map/all_gather | solution.py:122
  513.6 3.9 convolution_convert_fusion
  (47 shorter events, 1.2 us)
Async XLA Ops:
  7.2 140.2 %all-gather.10.cloned.1.call-start = ((), (), s32[]{:S(2)}) async-start(), calls=%async_computation.2 | async-start | bytes 2129920 | tf_op jit(solution)/shard_map/all_gather | solution.py:88
  7.9 186.5 %all-gather.6.cloned.1.call-start = ((), (), s32[]{:S(2)}) async-start(), calls=%async_computation | async-start | bytes 3538944 | tf_op jit(solution)/shard_map/all_gather | solution.py:57
  8.6 323.8 %all-gather.8.cloned.1.call-start = ((), (), s32[]{:S(2)}) async-start(), calls=%async_computation.1 | async-start | bytes 3194880 | tf_op jit(solution)/shard_map/all_gather | solution.py:63
  9.4 459.6 %all-gather.14.cloned.1.call-start = ((), (), s32[]{:S(2)}) async-start(), calls=%async_computation.4 | async-start | bytes 1064960 | tf_op jit(solution)/shard_map/all_gather | solution.py:126
  10.0 503.6 %all-gather.12.cloned.1.call-start = ((), (), s32[]{:S(2)}) async-start(), calls=%async_computation.3 | async-start | bytes 3538944 | tf_op jit(solution)/shard_map/all_gather | solution.py:122
  162.6 174.6 %copy-start.4 = (f32[2048]{0:T(1024)S(1)}, f32[2048]{0:T(1024)}, u32[]{:S(2)}) copy-start(f32[2048]{0:T(1024)} %param.13) | copy-start | bytes 24580
  194.4 142.7 %copy-start = (bf16[768,2048]{1,0:T(8,128)(2,1)S(1)}, bf16[768,2048]{1,0:T(8,128)(2,1)}, u32[]{:S(2)}) copy-start(bf16[768,2048]{1,0:T(8,128)(2,1)} %all-gather.6.cloned.1.call-done) | copy-start | bytes 9437188
  341.8 5.7 %copy-start.2 = (f32[768,3,4,64]{0,3,2,1:T(8,128)}, f32[768,3,4,64]{0,3,2,1:T(8,128)S(1)}, u32[]{:S(2)}) copy-start(f32[768,3,4,64]{0,3,2,1:T(8,128)S(1)} %fusion.34) | copy-start | bytes 7077892
  341.8 1.5 copy-start.1
  350.2 1.3 copy-start.3
Sparse Core Ops, SparseCore 0:
  10.9 136.3 all-gather.9
  149.5 44.9 all-gather.5
  197.4 134.9 all-gather.7
  335.2 133.7 all-gather.13
  471.5 42.0 all-gather.11
where the time goes:
time: 525 us; the launch traced here: 524 us
  waiting for transfers between devices  436 us (83%)
  local copies, waits for them, and re-layouts  32.3 us (6%)
  matrix products  20.6 us (4%)
  other arithmetic  19.5 us (4%)
  between operations  15.3 us (3%)
    all_gather x1, waiting for transfers between devices, local(): prefix_whole = lax.all_gather(prefix_pool, 'wide', axis=0, tiled=True)  134 us
    all_gather x1, waiting for transfers between devices, local(): piece_rows = lax.all_gather(qkv_weight, 'wide', axis=0, tiled=True)  133 us
    all_gather x1, waiting for transfers between devices, local(): lax.all_gather(out_weight, 'wide', axis=0, tiled=True)  90.2 us
    all_gather x1, waiting for transfers between devices, local(): all_heads = lax.all_gather(head_values, 'narrow', axis=1, tiled=True)  44.6 us
    all_gather x1, waiting for transfers between devices, local(): gathered = lax.all_gather(tokens, 'narrow', axis=1, tiled=True)  31.8 us
    reshape x2, local copies, waits for them, and re-layouts, local(): prefix_pages = prefix_whole.reshape(-1, PAGE, 2, heads_here, HEAD_DIM)  14.6 us
  transfers between devices with their start and end apart: 5, of which 5 were waited for; matrix products, arithmetic and copies ran while one was open for 13% of the time, Pallas kernels for 0%

commit v1 on v0

--- a/solution.py
+++ b/solution.py
@@ -123,7 +123,9 @@
     columns = all_heads
     branch_out = jnp.dot(
         columns,
-        lax.all_gather(out_weight, "wide", axis=0, tiled=True),
+        jnp.concatenate(
+            lax.all_to_all(jnp.stack([out_weight] * lax.axis_size("wide")), "wide", 0, 0), axis=0
+        ),
         preferred_element_type=jnp.float32,
     )
     return (branch_out.astype(jnp.bfloat16), new_pages)

time: 525 us -> 488 us (0.930)
  the two profiles are of different devices: /device:TPU:1 before, /device:TPU:38 now
where the time goes in v1:
time: 488 us; the launch traced here: 487 us
  waiting for transfers between devices  346 us (71%)
  starting transfers between devices  52.2 us (11%)
  local copies, waits for them, and re-layouts  33.5 us (7%)
  matrix products  20.6 us (4%)
  other arithmetic  19.5 us (4%)
  between operations  15.3 us (3%)
    all_gather x1, waiting for transfers between devices, local(): prefix_whole = lax.all_gather(prefix_pool, 'wide', axis=0, tiled=True)  142 us
    all_gather x1, waiting for transfers between devices, local(): piece_rows = lax.all_gather(qkv_weight, 'wide', axis=0, tiled=True)  140 us
    all_to_all x1, starting transfers between devices, local(): lax.all_to_all(jnp.stack([out_weight] * lax.axis_size('wide')), 'wide', 0...  52 us
    all_to_all x1, waiting for transfers between devices, local(): lax.all_to_all(jnp.stack([out_weight] * lax.axis_size('wide')), 'wide', 0...  38.7 us
    all_gather x1, waiting for transfers between devices, local(): gathered = lax.all_gather(tokens, 'narrow', axis=1, tiled=True)  23 us
    reshape x2, local copies, waits for them, and re-layouts, local(): prefix_pages = prefix_whole.reshape(-1, PAGE, 2, heads_here, HEAD_DIM)  14.6 us
  transfers between devices with their start and end apart: 5, of which 4 were waited for; matrix products, arithmetic and copies ran while one was open for 6% of the time, Pallas kernels for 0%

profile of v1, /device:TPU:38, one launch (start us, length us, event | category | flops | bytes accessed | tf_op | source)
XLA Modules:
  0.0 487.3 jit_solution(10673735141496898816)
XLA Ops:
  7.2 0.7 all-gather.9.cloned.1.call-update
  7.9 0.7 all-gather.5.cloned.1.call-update
  8.7 0.7 all-gather.7.cloned.1.call-update
  10.8 0.7 compare_and_fusion.1
  11.5 0.2 multiply_cosine_fusion
  11.7 1.0 iota_compare_fusion
  12.8 141.8 %all-gather.9.cloned.1.call-done = bf16[2048,2,256]{2,1,0:T(2,128)(2,1)} async-done(((bf16[32,2,256]{2,1,0:T(2,128)(2,1)}), bf16[2048,2,256]{2,1,0:T(2,128)(2,1)}) %all-gather.9.cloned.1.call-update) | async-done | bytes 2097168 | tf_op jit(solution)/shard_map/all_gather | solution.py:88
  154.6 8.8 %reshape.137 = bf16[16,128,2,4,64]{4,3,2,1,0:T(4,128)(2,1)} reshape(bf16[2048,2,256]{2,1,0:T(2,128)(2,1)} %all-gather.9.cloned.1.call-done) | data formatting | bytes 4194304 | tf_op jit(solution)/shard_map/reshape | solution.py:89
  163.4 5.8 %copy.32 = bf16[16,128,2,4,64]{1,4,3,2,0:T(8,128)(2,1)S(1)} copy(bf16[16,128,2,4,64]{4,3,2,1,0:T(4,128)(2,1)} %reshape.137) | data formatting | bytes 4194304 | tf_op jit(solution)/shard_map/reshape | solution.py:89
  169.2 0.6 gather_fusion.1
  169.8 23.0 %all-gather.5.cloned.1.call-done = bf16[768,2048]{1,0:T(8,128)(2,1)} async-done(((bf16[768,256]{1,0:T(8,128)(2,1)}), bf16[768,2048]{1,0:T(8,128)(2,1)}) %all-gather.5.cloned.1.call-update) | async-done | bytes 3145744 | tf_op jit(solution)/shard_map/all_gather | solution.py:57
  192.8 2.5 convert_reduce_fusion
  195.3 2.8 fusion.27
  198.2 140.4 %all-gather.7.cloned.1.call-done = bf16[2048,3,256]{2,0,1:T(8,128)(2,1)} async-done(((bf16[32,3,256]{2,0,1:T(8,128)(2,1)}), bf16[2048,3,256]{2,0,1:T(8,128)(2,1)}) %all-gather.7.cloned.1.call-update) | async-done | bytes 3145744 | tf_op jit(solution)/shard_map/all_gather | solution.py:63
  338.5 4.7 copy.30
  343.3 4.6 fusion.34
  347.9 0.1 slice_bitcast_fusion.4
  348.2 0.6 multiply_reduce_fusion
  348.9 0.5 copy-done.1
  349.4 1.8 fusion.22
  351.3 2.3 fusion.26
  353.6 2.8 fusion.57
  356.4 0.5 fusion.40
  356.9 0.7 fusion.51
  357.7 21.3 %while.15 = (s32[]{:T(128)}, f32[4,768]{1,0:T(4,128)S(1)}, f32[4,768]{1,0:T(4,128)S(1)}, f32[768,4,64]{0,2,1:T(8,128)S(1)}, s32[]{:T(128)}, /*index=5*/s32[]{:T(...) while((s32[]{:T(128)}, f32[4,768]{1,0:T(4,128)S(1)}, ...), condition=%wide.region_9.10_spmd.clone, body=%wide.region_6.9_spmd.clone.sunk | while | flops 423767072 | bytes 25763612 | solution.py:116
  357.7 0.7 fusion.88
  358.5 3.5 gather_fusion
  362.0 0.8 copy.47
  362.9 0.2 gather.23
  363.1 1.4 bitcast_reduce_fusion.2
  364.5 2.0 fusion.90
  366.5 1.7 fusion.91
  368.2 0.7 fusion.88
  369.0 3.5 gather_fusion
  372.5 0.8 copy.47
  373.4 0.2 gather.23
  373.6 1.4 bitcast_reduce_fusion.2
  375.0 2.0 fusion.90
  377.0 1.7 fusion.91
  379.0 0.8 divide_convert_fusion
  379.8 1.1 stack.4
  380.9 52.0 %all-to-all-start = ((bf16[64,32,256]{2,1,0:T(8,128)(2,1)}), bf16[64,32,256]{2,1,0:T(8,128)(2,1)}, u32[]{:S(2)}, u32[]{:S(2)}) async-start(bf16[64,32,256]{2,1,0:T(8,128)(2,1)} %stack.4), calls=%async_computation | async-start | bytes 2097152 | tf_op jit(solution)/shard_map/all_to_all | solution.py:127
  432.9 1.2 slice.106
  434.1 0.6 copy.37
  434.8 0.6 copy.36
  435.4 2.7 pad_maximum_fusion
  438.1 38.7 %all-to-all-done = bf16[64,32,256]{2,1,0:T(8,128)(2,1)} async-done(((bf16[64,32,256]{2,1,0:T(8,128)(2,1)}), bf16[64,32,256]{2,1,0:T(8,128)(2,1)}, u32[]{:S(2)}, u32[]{:S(2)}) %all-to-all-start) | async-done | bytes 1048608 | tf_op jit(solution)/shard_map/all_to_all | solution.py:127
  476.8 3.9 convolution_convert_fusion
  (49 shorter events, 1.1 us)
Async XLA Ops:
  7.2 147.4 %all-gather.9.cloned.1.call-start = ((), (), s32[]{:S(2)}) async-start(), calls=%async_computation.3 | async-start | bytes 2129920 | tf_op jit(solution)/shard_map/all_gather | solution.py:88
  7.9 184.9 %all-gather.5.cloned.1.call-start = ((), (), s32[]{:S(2)}) async-start(), calls=%async_computation.1 | async-start | bytes 3538944 | tf_op jit(solution)/shard_map/all_gather | solution.py:57
  8.6 329.9 %all-gather.7.cloned.1.call-start = ((), (), s32[]{:S(2)}) async-start(), calls=%async_computation.2 | async-start | bytes 3194880 | tf_op jit(solution)/shard_map/all_gather | solution.py:63
  9.4 467.4 %all-gather.11.cloned.1.call-start = ((), (), s32[]{:S(2)}) async-start(), calls=%async_computation.4 | async-start | bytes 3538944 | tf_op jit(solution)/shard_map/all_gather | solution.py:122
  169.8 173.5 %copy-start.5 = (f32[2048]{0:T(1024)S(1)}, f32[2048]{0:T(1024)}, u32[]{:S(2)}) copy-start(f32[2048]{0:T(1024)} %param.13) | copy-start | bytes 24580
  192.8 150.5 %copy-start = (bf16[768,2048]{1,0:T(8,128)(2,1)S(1)}, bf16[768,2048]{1,0:T(8,128)(2,1)}, u32[]{:S(2)}) copy-start(bf16[768,2048]{1,0:T(8,128)(2,1)} %all-gather.5.cloned.1.call-done) | copy-start | bytes 9437188
  347.9 5.7 %copy-start.2 = (f32[768,3,4,64]{0,3,2,1:T(8,128)}, f32[768,3,4,64]{0,3,2,1:T(8,128)S(1)}, u32[]{:S(2)}) copy-start(f32[768,3,4,64]{0,3,2,1:T(8,128)S(1)} %fusion.34) | copy-start | bytes 7077892
  347.9 1.5 copy-start.1
  356.4 1.3 copy-start.4
  357.6 22.1 %copy-start.3 = (bf16[32,256]{1,0:T(8,128)(2,1)S(1)}, bf16[32,256]{1,0:T(8,128)(2,1)}, u32[]{:S(2)}) copy-start(bf16[32,256]{1,0:T(8,128)(2,1)} %param.15) | copy-start | bytes 49156
  380.9 95.9 %all-to-all-start = ((bf16[64,32,256]{2,1,0:T(8,128)(2,1)}), bf16[64,32,256]{2,1,0:T(8,128)(2,1)}, u32[]{:S(2)}, u32[]{:S(2)}) async-start(bf16[64,32,256]{2,1,0:T(8,128)(2,1)} %stack.4), calls=%async_computation | async-start | bytes 2097152 | tf_op jit(solution)/shard_map/all_to_all | solution.py:127
Sparse Core Ops, SparseCore 0:
  10.9 143.6 all-gather.8
  156.7 36.0 all-gather.4
  195.7 142.7 all-gather.6
  379.9 72.7 all-gather.10
